TPU v7x, 32 devices: a whole 2x2x4 slice. The times are simulated.
32 devices in a mesh: vol: 8 (over z, y), ptcl: 4 (over x, core).
Axes of the slice: x: 2, y: 2, z: 4, core: 2. Of those that a mesh axis runs over, the one named last changes fastest.
Arguments:
- images: bfloat16 [32, 256, 256], P(('vol', 'ptcl')), may hold values from -6 to 6
- defocus: bfloat16 [32], P(('vol', 'ptcl')), may hold values from 20 to 200
- volume: float32 [4096, 256], P('vol'), may hold values from -6 to 6
- counts: int32 [8, 4, 8], P('vol', 'ptcl'), may hold values from 1 to 96, as said below
- slot_pixel: int32 [8, 4, 8, 96], P('vol', 'ptcl'), may hold values from 0 to 511, as said below
- slot_taps: int32 [8, 4, 8, 8, 96], P('vol', 'ptcl'), may hold values from 0 to 511, as said below
- slot_weights: bfloat16 [8, 4, 8, 8, 96], P('vol', 'ptcl'), may hold values from 0.019897461 to 0.25
Outputs:
- volume_next: float32 [4096, 256], P('vol')
Inputs may be any that keep to these rules, and one draw needn't show every extreme that they name: The 8 counts of each holder sum to 512; in each particle shard one owner receives exactly 96 live slots from every holder of that shard. `slot_pixel`: the live slots of a holder (slot index below its count) name each of its 512 pixel blocks exactly once; the other slots hold valid ids. `slot_taps`: the 8 taps of one slot name 8 different blocks.
All inputs are finite; a program needn't handle non-finite values.
Results may differ from a plain program's by a relative error of at most 0.0034.
Values may be sent and summed in bfloat16 or wider, within the bound.
No kernel may reach another device: no remote copies, remote signals or barrier semaphores. Data moves between devices by JAX's collectives and lax.ppermute only.
A program may use at most 64 MiB of HBM per device.

v0:
```python
import math
import jax
import jax.numpy as jnp
from jax import lax
from jax.sharding import PartitionSpec as P

L = 256
BLK = 128
PB = 512
learn_rate = 1.0
phase_shift = 0.1


def dft_tables():
    freq_ids = jnp.arange(L, dtype=jnp.int32)
    product = (freq_ids[:, None] - L // 2) * freq_ids[None, :] % L
    angle = 2.0 * math.pi / L * product.astype(jnp.float32)
    return (jnp.cos(angle).astype(jnp.bfloat16), jnp.sin(angle).astype(jnp.bfloat16))


def transform(pictures, cos_table, sin_table):
    first = jnp.stack([cos_table, sin_table])
    rows = jnp.einsum("iyx,jkx->ijyk", pictures, first, preferred_element_type=jnp.float32).astype(
        jnp.bfloat16
    )
    count_img = pictures.shape[0]
    rows = rows.reshape(count_img, 2 * L, L)
    scale = jnp.asarray(1.0 / L, jnp.bfloat16)
    second = (
        jnp.concatenate(
            [
                jnp.concatenate([cos_table, -sin_table], axis=1),
                jnp.concatenate([-sin_table, -cos_table], axis=1),
            ],
            axis=0,
        )
        * scale
    )
    parts = jnp.einsum("ay,iyb->iab", second, rows, preferred_element_type=jnp.float32)
    parts = parts.reshape(count_img, 2, L, L // BLK, BLK)
    blocks = jnp.transpose(parts, (0, 2, 3, 1, 4))
    return blocks.reshape(count_img * PB, 2 * BLK).astype(jnp.bfloat16)


def ctf_rows(block_id, focus):
    row_id = block_id // (L // BLK)
    col_id = block_id % (L // BLK) * BLK
    lane_ids = jnp.arange(BLK, dtype=jnp.int32)
    freq_y = (row_id - L // 2).astype(jnp.float32) / L
    freq_x = (col_id[..., None] + lane_ids - L // 2).astype(jnp.float32) / L
    radius = freq_x * freq_x + (freq_y * freq_y)[..., None]
    return -jnp.sin(math.pi * focus.astype(jnp.float32)[..., None] * radius + phase_shift)


def residual_terms(prediction, observed, ctf_values, live_slots):
    shape = prediction.shape
    pred_wide = prediction.astype(jnp.float32).reshape(shape[:-1] + (2, BLK))
    obs_wide = observed.astype(jnp.float32).reshape(shape[:-1] + (2, BLK))
    factor = ctf_values[..., None, :]
    misfit = factor * (factor * pred_wide - obs_wide)
    misfit = jnp.where(live_slots[..., None, None], misfit, 0.0)
    return misfit.reshape(shape).astype(jnp.bfloat16)


def tap_matrix(tap_ids, weights, block_count):
    owners, taps, slots = tap_ids.shape
    flat_taps = jnp.transpose(tap_ids, (0, 2, 1)).reshape(owners * slots, taps)
    flat_weights = jnp.transpose(weights, (0, 2, 1)).reshape(owners * slots, taps)
    block_ids = jnp.arange(block_count, dtype=jnp.int32)
    picked = jnp.where(
        flat_taps[:, :, None] == block_ids[None, None, :],
        flat_weights[:, :, None],
        jnp.zeros((), jnp.bfloat16),
    )
    return jnp.sum(picked, axis=1, dtype=jnp.bfloat16)


def local(images, defocus, volume, counts, slot_pixel, slot_taps, slot_weights):
    cos_table, sin_table = dft_tables()
    extract = volume.astype(jnp.bfloat16)
    slot_count = counts[0, 0]
    pixel_ids = slot_pixel[0, 0]
    tap_ids = slot_taps[0, 0]
    weights = slot_weights[0, 0]
    owners, taps, capacity = tap_ids.shape
    live_slots = jnp.arange(capacity, dtype=jnp.int32)[None, :] < slot_count[:, None]
    meta = jnp.concatenate(
        [
            tap_ids.astype(jnp.float32),
            weights.astype(jnp.float32),
            (pixel_ids % PB).astype(jnp.float32)[:, None, :],
            defocus[pixel_ids // PB].astype(jnp.float32)[:, None, :],
            live_slots.astype(jnp.float32)[:, None, :],
        ],
        axis=1,
    )
    got_meta = lax.all_to_all(meta, "vol", split_axis=0, concat_axis=0, tiled=True)
    observed = transform(images, cos_table, sin_table)
    rows = observed[pixel_ids]
    got_rows = lax.all_to_all(rows, "vol", split_axis=0, concat_axis=0, tiled=True)
    got_taps = got_meta[:, :taps, :].astype(jnp.int32)
    got_weights = got_meta[:, taps : 2 * taps, :].astype(jnp.bfloat16)
    got_block = got_meta[:, 2 * taps, :].astype(jnp.int32)
    got_focus = got_meta[:, 2 * taps + 1, :]
    got_live = got_meta[:, 2 * taps + 2, :] > 0.5
    matrix = tap_matrix(got_taps, got_weights, volume.shape[0])
    prediction = jnp.dot(matrix, extract, preferred_element_type=jnp.float32)
    prediction = prediction.astype(jnp.bfloat16).reshape(owners, capacity, -1)
    ctf_values = ctf_rows(got_block, got_focus)
    weighted = residual_terms(prediction, got_rows, ctf_values, got_live)
    flat_residual = weighted.reshape(-1, volume.shape[1])
    gradient = lax.dot_general(
        matrix, flat_residual, (((0,), (0,)), ((), ())), preferred_element_type=jnp.float32
    )
    gradient = lax.psum(gradient, "ptcl")
    return volume - learn_rate * gradient


def solution(mesh):
    placed = (
        P(("vol", "ptcl"), None, None),
        P(("vol", "ptcl")),
        P("vol", None),
        P("vol", "ptcl", None),
        P("vol", "ptcl", None, None),
        P("vol", "ptcl", None, None, None),
        P("vol", "ptcl", None, None, None),
    )
    return jax.shard_map(
        local, mesh=mesh, in_specs=placed, out_specs=P("vol", None), check_vma=False
    )
```

profile of v0, /device:TPU:0, one launch (start us, length us, event | category | flops | bytes accessed | tf_op | source)
XLA Modules:
  0.0 89.9 jit_solution(17016676902778621159)
XLA Ops:
  7.2 0.7 compare_convert_fusion
  8.0 0.7 fusion.40
  8.7 0.8 convert_bitcast_fusion
  9.4 0.7 bitcast_convert_fusion
  10.2 1.9 %concatenate.12 = f32[8,19,96]{2,1,0:T(8,128)} concatenate(f32[8,8,96]{2,1,0:T(8,128)S(1)} %convert_bitcast_fusion, f32[8,8,96]{2,1,0:T(8,128)S(1)} %bitcast_convert_fusion, f32[8,1,96]{2,1,0:T(1,128)S(1)} %fusion.40, f32[8,1,96]{2,1,0:T(1,128)S(1)} %gather.6, f32[8,1,96]{2,1,0:T(1,128)S(1)} %compare_convert_fusion), dimensions={1} | concatenate | bytes 116736 | tf_op jit(solution)/shard_map/concatenate | solution.py:87
  12.0 7.3 %all-to-all-start = ((f32[8,19,96]{2,1,0:T(8,128)}), f32[8,19,96]{2,1,0:T(8,128)S(1)}, u32[]{:S(2)}, u32[]{:S(2)}) async-start(f32[8,19,96]{2,1,0:T(8,128)} %concatenate.12), calls=%async_computation | async-start | bytes 196608 | tf_op jit(solution)/shard_map/all_to_all | solution.py:97
  19.3 0.7 compare_select_fusion.2
  20.0 1.1 %cosine_convert_fusion = bf16[256,256]{1,0:T(8,128)(2,1)S(1)} fusion(s32[256]{0:T(256)S(1)} %iota_add_fusion), kind=kLoop, calls=%fused_computation.39 | loop fusion | flops 983040 | bytes 132096 | tf_op jit(solution)/shard_map/convert_element_type | solution.py:18
  21.1 1.3 %fusion.30 = (bf16[256,256]{1,0:T(8,128)(2,1)S(1)}, bf16[256,256]{1,0:T(8,128)(2,1)S(1)}) fusion(s32[256]{0:T(256)S(1)} %iota_add_fusion), kind=kLoop, calls=%fused_computation.49 | loop fusion | flops 1441792 | bytes 263168 | tf_op jit(solution)/shard_map/neg | solution.py:32
  22.4 1.3 %cosine_convert_fusion.1 = (bf16[1,256,256]{2,1,0:T(8,128)(2,1)S(1)}, bf16[1,256,256]{2,1,0:T(8,128)(2,1)S(1)}) fusion(s32[256]{0:T(256)S(1)} %iota_add_fusion), kind=kLoop, calls=%fused_computation.43 | loop fusion | flops 1048576 | bytes 263168 | tf_op jit(solution)/shard_map/convert_element_type | solution.py:18
  24.0 0.4 fusion.2
  24.4 0.5 copy.25
  25.0 3.3 %gather_fusion = bf16[768,256]{1,0:T(8,128)(2,1)} fusion(bf16[512,256]{1,0:T(8,128)(2,1)S(1)} %bitcast.54, s32[1024]{0:T(1024)S(1)} %pad_clamp_fusion), kind=kCustom, calls=%fused_computation | custom fusion | bytes 789504 | tf_op jit(solution)/shard_map/gather | solution.py:99
  28.2 6.0 %all-to-all-start.1 = ((bf16[8,96,256]{2,1,0:T(8,128)(2,1)}), bf16[8,96,256]{2,1,0:T(8,128)(2,1)S(1)}, u32[]{:S(2)}, u32[]{:S(2)}) async-start(bf16[8,96,256]{2,1,0:T(8,128)(2,1)} %bitcast.22), calls=%async_computation.1 | async-start | bytes 786432 | tf_op jit(solution)/shard_map/all_to_all | solution.py:100
  34.7 5.1 %fusion.1 = bf16[768,512]{1,0:T(8,128)(2,1)S(1)} fusion(s32[768,8]{1,0:T(8,128)S(1)} %bitcast.56, bf16[768,8]{1,0:T(8,128)(2,1)S(1)} %bitcast.59), kind=kLoop, calls=%fused_computation.3 | loop fusion | flops 9043968 | bytes 823296 | tf_op jit(solution)/shard_map/reduce_sum | solution.py:75
  39.7 3.6 %sine_negate_fusion = f32[8,96,128]{2,1,0:T(8,128)S(1)} fusion(f32[8,96]{1,0:T(8,128)S(1)} %fusion.39, s32[8,96]{1,0:T(8,128)S(1)} %fusion.35, f32[8,96]{1,0:T(8,128)S(1)} %bitcast.63), kind=kLoop, calls=%fused_computation.26 | loop fusion | flops 884736 | bytes 402432 | tf_op jit(solution)/shard_map/neg | solution.py:52
  43.3 0.3 mul.162
  43.6 0.6 mul.163
  44.3 0.4 copy-done.1
  44.6 0.4 convolution_convert_fusion
  45.0 0.3 all-to-all-done.1
  45.5 1.2 %fusion.48 = f32[512,256]{1,0:T(8,128)} fusion(bf16[768,512]{1,0:T(8,128)(2,1)S(1)} %fusion.1, bf16[768,256]{1,0:T(8,128)(2,1)S(1)} %bitcast.60), kind=kOutput, calls=%fused_computation.87 | convolution fusion | flops 201326592 | bytes 1703936 | tf_op jit(solution)/shard_map/dot_general | solution.py:112
  46.8 34.4 %all-reduce.2.cloned.1.call-done = f32[512,256]{1,0:T(8,128)} async-done(((f32[512,256]{1,0:T(8,128)}), f32[512,256]{1,0:T(8,128)}) %all-reduce.2.cloned.1.call-update) | async-done | bytes 524304 | tf_op jit(solution)/shard_map/psum | solution.py:115
  81.2 1.9 %sub.41 = f32[512,256]{1,0:T(8,128)} subtract(f32[512,256]{1,0:T(8,128)S(1)} %copy-done.1, f32[512,256]{1,0:T(8,128)} %all-reduce.2.cloned.1.call-done) | non-fusion elementwise | flops 131072 | bytes 1572864 | tf_op jit(solution)/shard_map/sub | solution.py:116
  (22 shorter events, 1.1 us)
Async XLA Ops:
  6.5 17.2 %copy-start = (bf16[1,256,256]{2,1,0:T(8,128)(2,1)S(1)}, bf16[1,256,256]{2,1,0:T(8,128)(2,1)}, u32[]{:S(2)}) copy-start(bf16[1,256,256]{2,1,0:T(8,128)(2,1)} %param.7) | copy-start | bytes 393220
  12.0 16.2 %all-to-all-start = ((f32[8,19,96]{2,1,0:T(8,128)}), f32[8,19,96]{2,1,0:T(8,128)S(1)}, u32[]{:S(2)}, u32[]{:S(2)}) async-start(f32[8,19,96]{2,1,0:T(8,128)} %concatenate.12), calls=%async_computation | async-start | bytes 196608 | tf_op jit(solution)/shard_map/all_to_all | solution.py:97
  28.2 17.1 %all-to-all-start.1 = ((bf16[8,96,256]{2,1,0:T(8,128)(2,1)}), bf16[8,96,256]{2,1,0:T(8,128)(2,1)S(1)}, u32[]{:S(2)}, u32[]{:S(2)}) async-start(bf16[8,96,256]{2,1,0:T(8,128)(2,1)} %bitcast.22), calls=%async_computation.1 | async-start | bytes 786432 | tf_op jit(solution)/shard_map/all_to_all | solution.py:100
  34.2 46.9 %all-reduce.2.cloned.1.call-start = ((), (), s32[]{:S(2)}) async-start(), calls=%async_computation.2 | async-start | bytes 1048576 | tf_op jit(solution)/shard_map/psum | solution.py:115
  43.6 1.0 %copy-start.1 = (f32[512,256]{1,0:T(8,128)S(1)}, f32[512,256]{1,0:T(8,128)}, u32[]{:S(2)}) copy-start(f32[512,256]{1,0:T(8,128)} %param.9) | copy-start | bytes 1572868
Sparse Core Ops, SparseCore 0:
  46.9 34.2 all-reduce.1
where the time goes:
time: 90.5 us; the launch traced here: 89.9 us
  waiting for transfers between devices  34.8 us (38%)
  other arithmetic  18 us (20%)
  between operations  14.3 us (16%)
  starting transfers between devices  13.3 us (15%)
  local copies, waits for them, and re-layouts  7.42 us (8%)
  matrix products  2.18 us (2%)
    psum x1, waiting for transfers between devices, local(): gradient = lax.psum(gradient, 'ptcl')  34.4 us
    all_to_all x1, starting transfers between devices, local(): lax.all_to_all(meta, 'vol', split_axis=0, concat_axis=0, tiled=True)  7.28 us
    all_to_all x1, starting transfers between devices, local(): lax.all_to_all(rows, 'vol', split_axis=0, concat_axis=0, tiled=True)  5.99 us
    reduce_sum x1, other arithmetic, tap_matrix(): return jnp.sum(picked, axis=1, dtype=jnp.bfloat16)  5.06 us
    neg x1, other arithmetic, ctf_rows(): -jnp.sin(math.pi * focus.astype(jnp.float32)[..., None] * radius + phase_...  3.56 us
    gather x1, local copies, waits for them, and re-layouts, local(): rows = observed[pixel_ids]  3.28 us
    convert_element_type x2, other arithmetic, dft_tables(): jnp.cos(angle).astype(jnp.bfloat16)  2.31 us
    sub x1, other arithmetic, local(): return volume - learn_rate * gradient  1.9 us
  transfers between devices with their start and end apart: 3, of which 2 were waited for; matrix products, arithmetic and copies ran while one was open for 21% of the time, Pallas kernels for 0%

commit v1 on v0

--- a/solution.py
+++ b/solution.py
@@ -112,7 +112,7 @@
     gradient = lax.dot_general(
         matrix, flat_residual, (((0,), (0,)), ((), ())), preferred_element_type=jnp.float32
     )
-    gradient = lax.psum(gradient, "ptcl")
+    gradient = jnp.sum(lax.all_gather(gradient, "ptcl"), axis=0)
     return volume - learn_rate * gradient
 
 

time: 90.5 us -> 80.2 us (0.89)
  waiting for transfers between devices: 34.8 us -> 24.1 us
    psum x1 -> x0, waiting for transfers between devices: 34.4 us -> none  [local(): gradient = lax.psum(gradient, 'ptcl')]
    all_gather x0 -> x1, waiting for transfers between devices: none -> 23.4 us  [local(): gradient = jnp.sum(lax.all_gather(gradient, 'ptcl'), axis=0)]
    reduce_sum x0 -> x1, other arithmetic: none -> 1.79 us  [local(): gradient = jnp.sum(lax.all_gather(gradient, 'ptcl'), axis=0)]
    sub x1, other arithmetic: 1.9 us -> 0.86 us  [local(): return volume - learn_rate * gradient]
  transfers between devices with their start and end apart: 3 -> 3, of which waited for: 2 -> 2; matrix products, arithmetic and copies ran while one was open for 21% -> 24% of each run, Pallas kernels for 0% -> 0%
where the time goes in v1:
time: 80.2 us; the launch traced here: 79.7 us
  waiting for transfers between devices  24.1 us (30%)
  other arithmetic  18.7 us (23%)
  between operations  14.3 us (18%)
  starting transfers between devices  13.3 us (17%)
  local copies, waits for them, and re-layouts  7.04 us (9%)
  matrix products  2.18 us (3%)
    all_gather x1, waiting for transfers between devices, local(): gradient = jnp.sum(lax.all_gather(gradient, 'ptcl'), axis=0)  23.4 us
    all_to_all x1, starting transfers between devices, local(): lax.all_to_all(meta, 'vol', split_axis=0, concat_axis=0, tiled=True)  7.28 us
    all_to_all x1, starting transfers between devices, local(): lax.all_to_all(rows, 'vol', split_axis=0, concat_axis=0, tiled=True)  5.99 us
    reduce_sum x1, other arithmetic, tap_matrix(): return jnp.sum(picked, axis=1, dtype=jnp.bfloat16)  5.06 us
    neg x1, other arithmetic, ctf_rows(): -jnp.sin(math.pi * focus.astype(jnp.float32)[..., None] * radius + phase_...  3.56 us
    gather x1, local copies, waits for them, and re-layouts, local(): rows = observed[pixel_ids]  3.28 us
    convert_element_type x2, other arithmetic, dft_tables(): jnp.cos(angle).astype(jnp.bfloat16)  2.31 us
    concatenate x1, local copies, waits for them, and re-layouts, local(): jnp.concatenate([tap_ids.astype(jnp.float32), weights.astype(jnp.float32)...  1.87 us
  transfers between devices with their start and end apart: 3, of which 2 were waited for; matrix products, arithmetic and copies ran while one was open for 24% of the time, Pallas kernels for 0%

profile of v1, /device:TPU:0, one launch (start us, length us, event | category | flops | bytes accessed | tf_op | source)
XLA Modules:
  0.0 79.7 jit_solution(8814417764922895563)
XLA Ops:
  7.2 0.7 compare_convert_fusion
  8.0 0.7 fusion.40
  8.7 0.8 convert_bitcast_fusion
  9.4 0.7 bitcast_convert_fusion
  10.2 1.9 %concatenate.12 = f32[8,19,96]{2,1,0:T(8,128)} concatenate(f32[8,8,96]{2,1,0:T(8,128)S(1)} %convert_bitcast_fusion, f32[8,8,96]{2,1,0:T(8,128)S(1)} %bitcast_convert_fusion, f32[8,1,96]{2,1,0:T(1,128)S(1)} %fusion.40, f32[8,1,96]{2,1,0:T(1,128)S(1)} %gather.6, f32[8,1,96]{2,1,0:T(1,128)S(1)} %compare_convert_fusion), dimensions={1} | concatenate | bytes 116736 | tf_op jit(solution)/shard_map/concatenate | solution.py:87
  12.0 7.3 %all-to-all-start = ((f32[8,19,96]{2,1,0:T(8,128)}), f32[8,19,96]{2,1,0:T(8,128)S(1)}, u32[]{:S(2)}, u32[]{:S(2)}) async-start(f32[8,19,96]{2,1,0:T(8,128)} %concatenate.12), calls=%async_computation | async-start | bytes 196608 | tf_op jit(solution)/shard_map/all_to_all | solution.py:97
  19.3 0.7 compare_select_fusion.2
  20.0 1.1 %cosine_convert_fusion = bf16[256,256]{1,0:T(8,128)(2,1)S(1)} fusion(s32[256]{0:T(256)S(1)} %iota_add_fusion), kind=kLoop, calls=%fused_computation.39 | loop fusion | flops 983040 | bytes 132096 | tf_op jit(solution)/shard_map/convert_element_type | solution.py:18
  21.1 1.3 %fusion.30 = (bf16[256,256]{1,0:T(8,128)(2,1)S(1)}, bf16[256,256]{1,0:T(8,128)(2,1)S(1)}) fusion(s32[256]{0:T(256)S(1)} %iota_add_fusion), kind=kLoop, calls=%fused_computation.49 | loop fusion | flops 1441792 | bytes 263168 | tf_op jit(solution)/shard_map/neg | solution.py:32
  22.4 1.3 %cosine_convert_fusion.1 = (bf16[1,256,256]{2,1,0:T(8,128)(2,1)S(1)}, bf16[1,256,256]{2,1,0:T(8,128)(2,1)S(1)}) fusion(s32[256]{0:T(256)S(1)} %iota_add_fusion), kind=kLoop, calls=%fused_computation.43 | loop fusion | flops 1048576 | bytes 263168 | tf_op jit(solution)/shard_map/convert_element_type | solution.py:18
  24.0 0.4 fusion.2
  24.4 0.5 copy.25
  25.0 3.3 %gather_fusion = bf16[768,256]{1,0:T(8,128)(2,1)} fusion(bf16[512,256]{1,0:T(8,128)(2,1)S(1)} %bitcast.55, s32[1024]{0:T(1024)S(1)} %pad_clamp_fusion), kind=kCustom, calls=%fused_computation | custom fusion | bytes 789504 | tf_op jit(solution)/shard_map/gather | solution.py:99
  28.2 6.0 %all-to-all-start.1 = ((bf16[8,96,256]{2,1,0:T(8,128)(2,1)}), bf16[8,96,256]{2,1,0:T(8,128)(2,1)S(1)}, u32[]{:S(2)}, u32[]{:S(2)}) async-start(bf16[8,96,256]{2,1,0:T(8,128)(2,1)} %bitcast.22), calls=%async_computation.1 | async-start | bytes 786432 | tf_op jit(solution)/shard_map/all_to_all | solution.py:100
  34.7 5.1 %fusion.1 = bf16[768,512]{1,0:T(8,128)(2,1)S(1)} fusion(s32[768,8]{1,0:T(8,128)S(1)} %bitcast.58, bf16[768,8]{1,0:T(8,128)(2,1)S(1)} %bitcast.61), kind=kLoop, calls=%fused_computation.3 | loop fusion | flops 9043968 | bytes 823296 | tf_op jit(solution)/shard_map/reduce_sum | solution.py:75
  39.8 3.6 %sine_negate_fusion = f32[8,96,128]{2,1,0:T(8,128)S(1)} fusion(f32[8,96]{1,0:T(8,128)S(1)} %fusion.39, s32[8,96]{1,0:T(8,128)S(1)} %fusion.35, f32[8,96]{1,0:T(8,128)S(1)} %bitcast.65), kind=kLoop, calls=%fused_computation.26 | loop fusion | flops 884736 | bytes 402432 | tf_op jit(solution)/shard_map/neg | solution.py:52
  43.3 0.3 mul.162
  43.6 0.6 mul.163
  44.3 0.4 convolution_convert_fusion
  44.6 0.7 all-to-all-done.1
  45.5 1.2 %fusion.48 = f32[512,256]{1,0:T(8,128)} fusion(bf16[768,512]{1,0:T(8,128)(2,1)S(1)} %fusion.1, bf16[768,256]{1,0:T(8,128)(2,1)S(1)} %bitcast.62), kind=kOutput, calls=%fused_computation.87 | convolution fusion | flops 201326592 | bytes 1703936 | tf_op jit(solution)/shard_map/dot_general | solution.py:112
  46.8 23.4 %all-gather.3.cloned.1.call-done = f32[2048,256]{1,0:T(8,128)} async-done(((f32[512,256]{1,0:T(8,128)}), f32[2048,256]{1,0:T(8,128)}) %all-gather.3.cloned.1.call-update) | async-done | bytes 2097168 | tf_op jit(solution)/shard_map/all_gather | solution.py:115
  70.2 1.8 %reduce_sum.19 = f32[512,256]{1,0:T(8,128)S(1)} reduce(f32[4,512,256]{2,1,0:T(8,128)} %bitcast.56, f32[]{:T(128)} %constant.88.clone.1), dimensions={0}, to_apply=%region_1.2 | reduce | flops 393216 | bytes 2621444 | tf_op jit(solution)/shard_map/reduce_sum | solution.py:115
  72.0 0.9 %sub.41 = f32[512,256]{1,0:T(8,128)} subtract(f32[512,256]{1,0:T(8,128)S(1)} %copy-done.1, f32[512,256]{1,0:T(8,128)S(1)} %reduce_sum.19) | non-fusion elementwise | flops 131072 | bytes 1572864 | tf_op jit(solution)/shard_map/sub | solution.py:116
  (23 shorter events, 1.1 us)
Async XLA Ops:
  6.5 17.2 %copy-start = (bf16[1,256,256]{2,1,0:T(8,128)(2,1)S(1)}, bf16[1,256,256]{2,1,0:T(8,128)(2,1)}, u32[]{:S(2)}) copy-start(bf16[1,256,256]{2,1,0:T(8,128)(2,1)} %param.7) | copy-start | bytes 393220
  12.0 16.2 %all-to-all-start = ((f32[8,19,96]{2,1,0:T(8,128)}), f32[8,19,96]{2,1,0:T(8,128)S(1)}, u32[]{:S(2)}, u32[]{:S(2)}) async-start(f32[8,19,96]{2,1,0:T(8,128)} %concatenate.12), calls=%async_computation | async-start | bytes 196608 | tf_op jit(solution)/shard_map/all_to_all | solution.py:97
  28.2 17.1 %all-to-all-start.1 = ((bf16[8,96,256]{2,1,0:T(8,128)(2,1)}), bf16[8,96,256]{2,1,0:T(8,128)(2,1)S(1)}, u32[]{:S(2)}, u32[]{:S(2)}) async-start(bf16[8,96,256]{2,1,0:T(8,128)(2,1)} %bitcast.22), calls=%async_computation.1 | async-start | bytes 786432 | tf_op jit(solution)/shard_map/all_to_all | solution.py:100
  34.2 35.9 %all-gather.3.cloned.1.call-start = ((), (), s32[]{:S(2)}) async-start(), calls=%async_computation.2 | async-start | bytes 2621440 | tf_op jit(solution)/shard_map/all_gather | solution.py:115
  34.7 9.6 %copy-start.1 = (f32[512,256]{1,0:T(8,128)S(1)}, f32[512,256]{1,0:T(8,128)}, u32[]{:S(2)}) copy-start(f32[512,256]{1,0:T(8,128)} %param.9) | copy-start | bytes 1572868
Sparse Core Ops, SparseCore 0:
  46.9 23.2 all-gather.2
